TPU v7x, 512 devices: a whole 4x4x16 slice. The times are simulated.
512 devices in a mesh: dp: 64 (over y, z), tensor: 8 (over x, core).
Axes of the slice: x: 4, y: 4, z: 16, core: 2. Of those that a mesh axis runs over, the one named last changes fastest.
Arguments:
- tokens: bfloat16 [65536, 1408], P(('dp', 'tensor')), may hold values from -6 to 6
- ln1_gain: float32 [1408], replicated, may hold values from 0.1 to 1.9
- ln1_shift: float32 [1408], replicated, may hold values from -3 to 3
- w_qkv: bfloat16 [1408, 16, 264], P(None, 'tensor')
- w_out: bfloat16 [16, 88, 1408], P('tensor'), may hold values from -0.625 to 0.625
- ln2_gain: float32 [1408], replicated, may hold values from 0.1 to 1.9
- ln2_shift: float32 [1408], replicated, may hold values from -3 to 3
- w_proj: bfloat16 [5632, 3584], P('dp', 'tensor'), may hold values from -0.078125 to 0.078125
- proj_bias: float32 [3584], P('tensor'), may hold values from -3 to 3
- segments: int32 [64, 256], P('dp'), may hold values from 0 to 7, never falling along the last dimension, each value on 1 to 128 neighbouring positions
- owners: int32 [16384, 1], P('dp'), may hold values from 0 to 63; in each aligned block of 256 rows (0 to 255, 256 to 511, ...) at most 8 rows name the same one
Outputs:
- delivered: bfloat16 [32768, 3584], P('dp', 'tensor')
Inputs may be any that keep to these rules, and one draw needn't show every extreme that they name: `segments`: within a pack numbers never fall, every image has 1 to 128 groups and one has exactly that many. `owners`: among the 256 merged tokens of one pack no owner gets more than 8; in some pack an owner gets exactly 8.
All inputs are finite; a program needn't handle non-finite values.
Results may differ from a plain program's by a relative error of at most 0.015.
Values may be sent and summed in bfloat16 or wider, within the bound.
No kernel may reach another device: no remote copies, remote signals or barrier semaphores. Data moves between devices by JAX's collectives and lax.ppermute only.
A program may use at most 64 MiB of HBM per device.

v0:
```python
import jax
import jax.numpy as jnp
from jax import lax
from jax.sharding import PartitionSpec as P


def layer_norm(values, gain, shift):
    wide = values.astype(jnp.float32)
    average = jnp.mean(wide, axis=-1, keepdims=True)
    centred = wide - average
    variance = jnp.mean(centred * centred, axis=-1, keepdims=True)
    return centred * lax.rsqrt(variance + 1e-06) * gain + shift


def attend(heads_qkv, token_segs):
    row_count = heads_qkv.shape[0]
    width = heads_qkv.shape[2] // 3
    queries = heads_qkv[:, :, :width]
    keys_all = heads_qkv[:, :, width : 2 * width]
    values_all = heads_qkv[:, :, 2 * width :]
    score_scale = 1.0 / jnp.sqrt(jnp.float32(width))
    block_rows = min(512, row_count)
    outputs = []
    for block_index in range(row_count // block_rows):
        lower = block_index * block_rows
        scores = (
            jnp.einsum(
                "qhd,khd->hqk",
                queries[lower : lower + block_rows],
                keys_all,
                preferred_element_type=jnp.float32,
            )
            * score_scale
        )
        same = token_segs[lower : lower + block_rows][:, None] == token_segs[None, :]
        scores = jnp.where(same[None], scores, -jnp.inf)
        row_max = jnp.max(scores, axis=-1, keepdims=True)
        exponent = jnp.exp(scores - row_max)
        probs = (exponent / jnp.sum(exponent, axis=-1, keepdims=True)).astype(jnp.bfloat16)
        context = jnp.einsum("hqk,khd->qhd", probs, values_all, preferred_element_type=jnp.float32)
        outputs.append(context.astype(jnp.bfloat16))
    return jnp.concatenate(outputs, axis=0)


def shards(
    tokens,
    ln1_gain,
    ln1_shift,
    w_qkv,
    w_out,
    ln2_gain,
    ln2_shift,
    w_proj,
    proj_bias,
    segments,
    owners,
):
    dp_count = lax.axis_size("dp")
    tp_count = lax.axis_size("tensor")
    w_proj_all = lax.all_gather(w_proj, "dp", axis=0, tiled=True)
    w_out_all = lax.all_gather(w_out, "tensor", axis=0, tiled=True)
    gathered = lax.all_gather(tokens, "tensor", axis=0, tiled=True)
    row_count = gathered.shape[0]
    local_rows = tokens.shape[0]
    normed = layer_norm(gathered, ln1_gain, ln1_shift).astype(jnp.bfloat16)
    heads_here = w_qkv.shape[1]
    heads_qkv = jnp.dot(
        normed, w_qkv.reshape(w_qkv.shape[0], -1), preferred_element_type=jnp.float32
    )
    heads_qkv = heads_qkv.astype(jnp.bfloat16).reshape(row_count, heads_here, -1)
    token_segs = jnp.repeat(segments[0], 4)
    context = attend(heads_qkv, token_segs).reshape(tp_count, local_rows, -1)
    context_mine = lax.all_to_all(context, "tensor", split_axis=0, concat_axis=0, tiled=True)
    out_heads = w_out_all.reshape(tp_count, -1, w_out_all.shape[2])
    attn = jnp.einsum("sqd,sdo->qo", context_mine, out_heads, preferred_element_type=jnp.float32)
    hidden = (tokens.astype(jnp.float32) + attn).astype(jnp.bfloat16)
    normed_two = layer_norm(hidden, ln2_gain, ln2_shift).astype(jnp.bfloat16)
    merged_mine = normed_two.reshape(local_rows // 4, -1)
    merged = lax.all_gather(merged_mine, "tensor", axis=0, tiled=True)
    groups = merged.shape[0]
    summed = jnp.dot(merged, w_proj_all, preferred_element_type=jnp.float32)
    projected = (summed + proj_bias).astype(jnp.bfloat16)
    dests = owners[:, 0]
    onehot = (dests[:, None] == jnp.arange(dp_count, dtype=jnp.int32)[None, :]).astype(jnp.int32)
    earlier = jnp.cumsum(onehot, axis=0) - onehot
    position = jnp.sum(earlier * onehot, axis=1)
    capacity = 2 * groups // dp_count
    slot_index = dests * capacity + position
    scatter_table = (
        slot_index[None, :] == jnp.arange(dp_count * capacity, dtype=jnp.int32)[:, None]
    ).astype(jnp.bfloat16)
    outgoing = jnp.dot(scatter_table, projected, preferred_element_type=jnp.float32).astype(
        jnp.bfloat16
    )
    outgoing = outgoing.reshape(dp_count, capacity, -1)
    arrived = lax.all_to_all(outgoing, "dp", split_axis=0, concat_axis=0, tiled=True)
    return arrived.reshape(dp_count * capacity, -1)


def solution(mesh):
    return jax.shard_map(
        shards,
        mesh=mesh,
        in_specs=(
            P(("dp", "tensor"), None),
            P(),
            P(),
            P(None, "tensor", None),
            P("tensor", None, None),
            P(),
            P(),
            P("dp", "tensor"),
            P("tensor"),
            P("dp", None),
            P("dp", None),
        ),
        out_specs=P("dp", "tensor"),
        check_vma=False,
    )
```

profile of v0, /device:TPU:8, one launch (start us, length us, event | category | flops | bytes accessed | tf_op | source)
XLA Modules:
  0.0 339.7 jit_solution(10978495204272725188)
XLA Ops:
  6.5 0.7 all-gather.5.cloned.1.call-update
  7.3 0.7 all-gather.7.cloned.1.call-update
  8.1 0.7 all-gather.11.cloned.1.call-update
  8.8 0.7 slice_bitcast_fusion.1
  9.9 0.8 broadcast_in_dim.25
  10.8 0.7 broadcast_compare_fusion.1
  11.4 36.8 %all-gather.5.cloned.1.call-done = bf16[1024,1408]{1,0:T(8,128)(2,1)} async-done(((bf16[128,1408]{1,0:T(8,128)(2,1)}), bf16[1024,1408]{1,0:T(8,128)(2,1)}) %all-gather.5.cloned.1.call-update) | async-done | bytes 2883600 | tf_op jit(solution)/shard_map/all_gather | solution.py:62
  48.2 2.4 convert_reduce_fusion
  50.9 0.9 fusion.4
  51.8 3.1 fusion.27
  55.0 4.8 %fusion.82 = (f32[2,512]{1,0:T(2,128)S(1)}, f32[2,512,1024]{2,1,0:T(8,128)}) fusion(pred[512,1024]{1,0:T(8,128)(4,1)S(1)} %get-tuple-element.5, bf16[1024,2,264]{0,2,1:T(8,128)(2,1)} %bitcast.63), kind=kOutput, calls=%fused_computation.86 | convolution fusion | flops 188744704 | bytes 5263360 | tf_op jit(solution)/shard_map/sub | solution.py:38
  59.8 4.8 %fusion.73 = (f32[2,512]{1,0:T(2,128)S(1)}, f32[2,512,1024]{2,1,0:T(8,128)}) fusion(pred[512,1024]{1,0:T(8,128)(4,1)S(1)} %get-tuple-element.6, bf16[1024,2,264]{0,2,1:T(8,128)(2,1)} %bitcast.64), kind=kOutput, calls=%fused_computation.85 | convolution fusion | flops 188744704 | bytes 5263360 | tf_op jit(solution)/shard_map/sub | solution.py:38
  64.6 3.2 fusion.33
  68.2 0.9 fusion.34
  69.3 16.0 %all_to_all.10 = bf16[8,128,176]{1,2,0:T(8,128)(2,1)S(1)} all-to-all(bf16[8,128,176]{1,2,0:T(8,128)(2,1)S(1)} %copy.18), channel_id=1, replica_groups=mesh['dp'=64,'tensor'=8] {'tensor'}, dimensions={0} | all-to-all | bytes 720896 | tf_op jit(solution)/shard_map/all_to_all | solution.py:73
  85.2 8.4 %all-gather.7.cloned.1.call-done = bf16[16,88,1408]{2,1,0:T(8,128)(2,1)} async-done(((bf16[2,88,1408]{2,1,0:T(8,128)(2,1)}), bf16[16,88,1408]{2,1,0:T(8,128)(2,1)}) %all-gather.7.cloned.1.call-update) | async-done | bytes 3964944 | tf_op jit(solution)/shard_map/all_gather | solution.py:61
  93.7 3.0 fusion.91
  97.1 1.0 reshape.155
  98.2 0.6 reduce-window.6
  99.1 146.7 %all-gather.11.cloned.1.call-done = bf16[5632,448]{1,0:T(8,128)(2,1)} async-done(((bf16[88,448]{1,0:T(8,128)(2,1)}), bf16[5632,448]{1,0:T(8,128)(2,1)}) %all-gather.11.cloned.1.call-update) | async-done | bytes 5046288 | tf_op jit(solution)/shard_map/all_gather | solution.py:60
  245.8 32.5 %all-gather.9.cloned.1.call-done = bf16[256,5632]{1,0:T(8,128)(2,1)} async-done(((bf16[32,5632]{1,0:T(8,128)(2,1)}), bf16[256,5632]{1,0:T(8,128)(2,1)}) %all-gather.9.cloned.1.call-update) | async-done | bytes 2883600 | tf_op jit(solution)/shard_map/all_gather | solution.py:79
  278.3 6.0 %convolution_convert_fusion = bf16[512,448]{0,1:T(8,128)(2,1)S(1)} fusion(bf16[256,5632]{1,0:T(8,128)(2,1)} %all-gather.9.cloned.1.call-done, bf16[5632,448]{1,0:T(8,128)(2,1)} %all-gather.11.cloned.1.call-done, s32[256]{0:T(256)S(1)} %multiply_add_fusion, f32[448]{0:T(512)S(1)} %copy-done.8), kind=kOutput, calls=%fused_computation.36 | convolution fusion | flops 1409875968 | bytes 8391424 | tf_op jit(solution)/shard_map/dot_general | solution.py:92
  284.5 47.7 %all_to_all.11 = bf16[64,8,448]{2,1,0:T(8,128)(2,1)S(1)} all-to-all(bf16[64,8,448]{2,1,0:T(8,128)(2,1)S(1)} %bitcast.55), channel_id=1, replica_groups=mesh['dp'=64,'tensor'=8] {'dp'}, dimensions={0} | all-to-all | bytes 917504 | tf_op jit(solution)/shard_map/all_to_all | solution.py:96
  332.2 1.0 copy.20
  (48 shorter events, 2.5 us)
Async XLA Ops:
  6.5 45.3 %copy-start = (bf16[1408,2,264]{0,2,1:T(8,128)(2,1)S(1)}, bf16[1408,2,264]{0,2,1:T(8,128)(2,1)}, u32[]{:S(2)}) copy-start(bf16[1408,2,264]{0,2,1:T(8,128)(2,1)} %param.14) | copy-start | bytes 4460548
  6.5 45.3 %copy-start.7 = (f32[1408]{0:T(1024)S(1)}, f32[1408]{0:T(1024)}, u32[]{:S(2)}) copy-start(f32[1408]{0:T(1024)} %param.12) | copy-start | bytes 16900
  6.5 45.3 %copy-start.6 = (f32[1408]{0:T(1024)S(1)}, f32[1408]{0:T(1024)}, u32[]{:S(2)}) copy-start(f32[1408]{0:T(1024)} %param.13) | copy-start | bytes 16900
  6.5 41.7 %all-gather.5.cloned.1.call-start = ((), (), s32[]{:S(2)}) async-start(), calls=%async_computation.2 | async-start | bytes 3244032 | tf_op jit(solution)/shard_map/all_gather | solution.py:62
  7.3 86.4 %all-gather.7.cloned.1.call-start = ((), (), s32[]{:S(2)}) async-start(), calls=%async_computation.3 | async-start | bytes 4460544 | tf_op jit(solution)/shard_map/all_gather | solution.py:61
  8.0 237.8 %all-gather.11.cloned.1.call-start = ((), (), s32[]{:S(2)}) async-start(), calls=%async_computation.5 | async-start | bytes 5857280 | tf_op jit(solution)/shard_map/all_gather | solution.py:60
  8.7 269.5 %all-gather.9.cloned.1.call-start = ((), (), s32[]{:S(2)}) async-start(), calls=%async_computation.4 | async-start | bytes 3244032 | tf_op jit(solution)/shard_map/all_gather | solution.py:79
  48.2 2.7 copy-start.1
  59.8 4.8 %copy-start.9 = (bf16[1024,528]{0,1:T(8,128)(2,1)S(1)}, bf16[1024,528]{0,1:T(8,128)(2,1)}, u32[]{:S(2)}) copy-start(bf16[1024,528]{0,1:T(8,128)(2,1)} %fusion.27) | copy-start | bytes 3244036
  64.6 3.6 %copy-start.10 = (f32[2,512,1024]{2,1,0:T(8,128)S(1)}, f32[2,512,1024]{2,1,0:T(8,128)}, u32[]{:S(2)}) copy-start(f32[2,512,1024]{2,1,0:T(8,128)} %get-tuple-element.10) | copy-start | bytes 12582916
  68.2 25.5 %copy-start.2 = (bf16[128,1408]{1,0:T(8,128)(2,1)S(1)}, bf16[128,1408]{1,0:T(8,128)(2,1)}, u32[]{:S(2)}) copy-start(bf16[128,1408]{1,0:T(8,128)(2,1)} %param.11) | copy-start | bytes 1081348
  69.1 27.8 %copy-start.4 = (f32[1408]{0:T(1024)S(1)}, f32[1408]{0:T(1024)}, u32[]{:S(2)}) copy-start(f32[1408]{0:T(1024)} %param.17) | copy-start | bytes 16900
  69.1 27.8 %copy-start.5 = (f32[1408]{0:T(1024)S(1)}, f32[1408]{0:T(1024)}, u32[]{:S(2)}) copy-start(f32[1408]{0:T(1024)} %param.16) | copy-start | bytes 16900
  85.2 12.9 %copy-start.3 = (s32[256,1]{0,1:T(1,128)S(1)}, s32[256,1]{0,1:T(1,128)}, u32[]{:S(2)}) copy-start(s32[256,1]{0,1:T(1,128)} %param.21) | copy-start | bytes 3076
  93.7 184.6 %copy-start.8 = (f32[448]{0:T(512)S(1)}, f32[448]{0:T(512)}, u32[]{:S(2)}) copy-start(f32[448]{0:T(512)} %param.19) | copy-start | bytes 5380
Sparse Core Ops, SparseCore 0:
  9.5 38.6 all-gather.4
  50.3 43.2 all-gather.6
  96.6 149.1 all-gather.10
  247.8 30.4 all-gather.8
where the time goes:
time: 340 us
  waiting for transfers between devices  226 us (66%)
  blocking collectives  63.7 us (19%)
  matrix products  25.8 us (8%)
  between operations  13.3 us (4%)
  other arithmetic  5.21 us (2%)
  local copies, waits for them, and re-layouts  5.09 us (1%)
    all_gather x1, waiting for transfers between devices, shards(): w_proj_all = lax.all_gather(w_proj, 'dp', axis=0, tiled=True)  147 us
    all_to_all x1, blocking collectives, shards(): lax.all_to_all(outgoing, 'dp', split_axis=0, concat_axis=0, tiled=True)  47.7 us
    all_gather x1, waiting for transfers between devices, shards(): gathered = lax.all_gather(tokens, 'tensor', axis=0, tiled=True)  36.8 us
    all_gather x1, waiting for transfers between devices, shards(): merged = lax.all_gather(merged_mine, 'tensor', axis=0, tiled=True)  32.5 us
    all_to_all x1, blocking collectives, shards(): lax.all_to_all(context, 'tensor', split_axis=0, concat_axis=0, tiled=True)  16 us
    sub x2, matrix products, attend(): exponent = jnp.exp(scores - row_max)  9.62 us
    all_gather x1, waiting for transfers between devices, shards(): w_out_all = lax.all_gather(w_out, 'tensor', axis=0, tiled=True)  8.44 us
  transfers between devices with their start and end apart: 4, of which 4 were waited for; matrix products, arithmetic and copies ran while one was open for 8% of the time, Pallas kernels for 0%

commit v1 on v0

--- a/solution.py
+++ b/solution.py
@@ -1,7 +1,42 @@
+import functools
 import jax
 import jax.numpy as jnp
 from jax import lax
 from jax.sharding import PartitionSpec as P
+
+
+def shards_link(x0, axis_no):
+    x0 = jnp.moveaxis(x0, 0, axis_no)
+    next_value = x0.shape
+    back = x0.reshape(
+        *next_value[:axis_no],
+        next_value[axis_no] * next_value[axis_no + 1],
+        *next_value[axis_no + 2 :]
+    )
+    return back
+
+
+def choose_loads(frame_in, axis_tag, along_dim):
+    parts_n = lax.axis_size(axis_tag)
+    fields = list(map(lambda num: (num, (num + 1) % parts_n), range(parts_n)))
+    sides = [(j, rr) for rr, j in fields]
+    far_arr, top = ([], [])
+    i = 0
+    while i < parts_n - 1:
+        if i % 2 == 0:
+            parts_out = lax.ppermute(far_arr[-1] if far_arr else frame_in, axis_tag, fields)
+            far_arr.append(parts_out)
+        else:
+            top.append(lax.ppermute(top[-1] if top else frame_in, axis_tag, sides))
+        i = i + 1
+    part_next = jnp.stack([*far_arr[::-1], frame_in, *top], axis=0)
+    mid_arr = lax.axis_index(axis_tag) - len(far_arr)
+    part_next = part_next[(jnp.arange(parts_n) - mid_arr) % parts_n]
+    clean = shards_link(part_next, along_dim)
+    return clean
+
+
+lay_entries = functools.partial(choose_loads, axis_tag="tensor", along_dim=0)
 
 
 def layer_norm(values, gain, shift):
@@ -59,7 +94,7 @@
     tp_count = lax.axis_size("tensor")
     w_proj_all = lax.all_gather(w_proj, "dp", axis=0, tiled=True)
     w_out_all = lax.all_gather(w_out, "tensor", axis=0, tiled=True)
-    gathered = lax.all_gather(tokens, "tensor", axis=0, tiled=True)
+    gathered = lay_entries(tokens)
     row_count = gathered.shape[0]
     local_rows = tokens.shape[0]
     normed = layer_norm(gathered, ln1_gain, ln1_shift).astype(jnp.bfloat16)

time: 340 us -> 304 us (0.89)
  waiting for transfers between devices: 226 us -> 169 us
  local copies, waits for them, and re-layouts: 5.09 us -> 20.4 us
  starting transfers between devices: 0.12 us -> 9.36 us
  blocking collectives: 63.7 us -> 58.7 us
    all_gather x1, waiting for transfers between devices: 147 us -> 107 us  [shards(): w_proj_all = lax.all_gather(w_proj, 'dp', axis=0, tiled=True)]
    all_gather x1 -> x0, waiting for transfers between devices: 36.8 us -> none  [shards(): gathered = lax.all_gather(tokens, 'tensor', axis=0, tiled=True)]
    ppermute x0 -> x7, waiting for transfers between devices: none -> 28.2 us  [the longest x4 23.8 us: choose_loads(): lax.ppermute(far_arr[-1] if far_arr else frame_in, axis_tag, fields)]
    unnamed x23 -> x30, local copies, waits for them, and re-layouts: 0.76 us -> 10.9 us
    ppermute x0 -> x7, starting transfers between devices: none -> 9.29 us  [the longest x3 9.26 us: choose_loads(): top.append(lax.ppermute(top[-1] if top else frame_in, axis_tag, sides))]
    all_gather x1, waiting for transfers between devices: 8.44 us -> 0.01 us  [shards(): w_out_all = lax.all_gather(w_out, 'tensor', axis=0, tiled=True)]
    all_to_all x1, blocking collectives: 16 us -> 11 us  [shards(): lax.all_to_all(context, 'tensor', split_axis=0, concat_axis=0, tiled=True)]
    gather x0 -> x1, local copies, waits for them, and re-layouts: none -> 4.33 us  [choose_loads(): part_next = part_next[(jnp.arange(parts_n) - mid_arr) % parts_n]]
  transfers between devices with their start and end apart: 4 -> 10, of which waited for: 4 -> 7; matrix products, arithmetic and copies ran while one was open for 8% -> 15% of each run, Pallas kernels for 0% -> 0%
where the time goes in v1:
time: 304 us
  waiting for transfers between devices  169 us (56%)
  blocking collectives  58.7 us (19%)
  matrix products  26.6 us (9%)
  local copies, waits for them, and re-layouts  20.4 us (7%)
  between operations  13.3 us (4%)
  starting transfers between devices  9.36 us (3%)
  other arithmetic  6.34 us (2%)
    all_gather x1, waiting for transfers between devices, shards(): w_proj_all = lax.all_gather(w_proj, 'dp', axis=0, tiled=True)  107 us
    all_to_all x1, blocking collectives, shards(): lax.all_to_all(outgoing, 'dp', split_axis=0, concat_axis=0, tiled=True)  47.7 us
    all_gather x1, waiting for transfers between devices, shards(): merged = lax.all_gather(merged_mine, 'tensor', axis=0, tiled=True)  32.6 us
    ppermute x4, waiting for transfers between devices, choose_loads(): lax.ppermute(far_arr[-1] if far_arr else frame_in, axis_tag, fields)  23.8 us
    all_to_all x1, blocking collectives, shards(): lax.all_to_all(context, 'tensor', split_axis=0, concat_axis=0, tiled=True)  11 us
    unnamed x30, local copies, waits for them, and re-layouts  10.9 us
    sub x2, matrix products, attend(): exponent = jnp.exp(scores - row_max)  9.54 us
    ppermute x3, starting transfers between devices, choose_loads(): top.append(lax.ppermute(top[-1] if top else frame_in, axis_tag, sides))  9.26 us
  transfers between devices with their start and end apart: 10, of which 7 were waited for; matrix products, arithmetic and copies ran while one was open for 15% of the time, Pallas kernels for 0%

profile of v1, /device:TPU:8, one launch (start us, length us, event | category | flops | bytes accessed | tf_op | source)
XLA Modules:
  0.0 303.7 jit_solution(14895337908173008195)
XLA Ops:
  7.3 8.3 %collective-permute-done = bf16[128,1408]{1,0:T(8,128)(2,1)S(1)} collective-permute-done((bf16[128,1408]{1,0:T(8,128)(2,1)}, bf16[128,1408]{1,0:T(8,128)(2,1)S(1)}, u32[]{:S(2)}, u32[]{:S(2)}) %collective-permute-start) | collective-permute-done | bytes 360480 | tf_op jit(solution)/shard_map/ppermute | solution.py:27
  15.6 3.0 collective-permute-start.4
  18.5 5.1 %collective-permute-done.1 = bf16[128,1408]{1,0:T(8,128)(2,1)S(1)} collective-permute-done((bf16[128,1408]{1,0:T(8,128)(2,1)S(1)}, bf16[128,1408]{1,0:T(8,128)(2,1)S(1)}, u32[]{:S(2)}, u32[]{:S(2)}) %collective-permute-start.1) | collective-permute-done | bytes 360480 | tf_op jit(solution)/shard_map/ppermute | solution.py:27
  25.8 2.9 collective-permute-start.5
  28.7 3.2 %collective-permute-done.2 = bf16[128,1408]{1,0:T(8,128)(2,1)} collective-permute-done((bf16[128,1408]{1,0:T(8,128)(2,1)S(1)}, bf16[128,1408]{1,0:T(8,128)(2,1)}, u32[]{:S(2)}, u32[]{:S(2)}) %collective-permute-start.2) | collective-permute-done | bytes 360480 | tf_op jit(solution)/shard_map/ppermute | solution.py:27
  32.5 4.4 %collective-permute-done.5 = bf16[128,1408]{1,0:T(8,128)(2,1)} collective-permute-done((bf16[128,1408]{1,0:T(8,128)(2,1)}, bf16[128,1408]{1,0:T(8,128)(2,1)}, u32[]{:S(2)}, u32[]{:S(2)}) %collective-permute-start.5) | collective-permute-done | bytes 360480 | tf_op jit(solution)/shard_map/ppermute | solution.py:30
  36.9 3.4 %collective-permute-start.6 = (bf16[128,1408]{1,0:T(8,128)(2,1)}, bf16[128,1408]{1,0:T(8,128)(2,1)S(1)}, u32[]{:S(2)}, u32[]{:S(2)}) collective-permute-start(bf16[128,1408]{1,0:T(8,128)(2,1)} %collective-permute-done.5), channel_id=1, source_target_pairs={{1,0},{2,1},{3,2},{4,3},{5,4},{6,5},{7,6},{0,7},{9,8},{10,9},{11,1... | collective-permute-start | bytes 1081352 | tf_op jit(solution)/shard_map/ppermute | solution.py:30
  40.3 7.3 %collective-permute-done.3 = bf16[128,1408]{1,0:T(8,128)(2,1)} collective-permute-done((bf16[128,1408]{1,0:T(8,128)(2,1)}, bf16[128,1408]{1,0:T(8,128)(2,1)}, u32[]{:S(2)}, u32[]{:S(2)}) %collective-permute-start.3) | collective-permute-done | bytes 360480 | tf_op jit(solution)/shard_map/ppermute | solution.py:27
  47.6 1.8 bitcast_dynamic-update-slice_fusion.7
  51.1 1.8 bitcast_dynamic-update-slice_fusion.5
  56.2 1.7 bitcast_dynamic-update-slice_fusion.1
  58.7 4.3 %gather_fusion = bf16[8,128,1408]{2,1,0:T(8,128)(2,1)} fusion(bf16[8,128,1408]{2,1,0:T(8,128)(2,1)} %bitcast_dynamic-update-slice_fusion, s32[1024]{0:T(1024)S(1)} %pad_clamp_fusion), kind=kCustom, calls=%fused_computation | custom fusion | bytes 5767200 | tf_op jit(solution)/shard_map/gather | solution.py:34
  63.1 2.4 convert_reduce_fusion
  67.8 2.9 convolution_convert_fusion
  70.7 4.8 %fusion.75 = (f32[2,512]{1,0:T(2,128)S(1)}, f32[2,512,1024]{2,1,0:T(8,128)}) fusion(pred[512,1024]{1,0:T(8,128)(4,1)S(1)} %get-tuple-element.5, bf16[1024,2,264]{0,2,1:T(8,128)(2,1)} %bitcast.84), kind=kOutput, calls=%fused_computation.97 | convolution fusion | flops 188744704 | bytes 5263360 | tf_op jit(solution)/shard_map/sub | solution.py:73
  75.5 4.7 %fusion.66 = (f32[2,512]{1,0:T(2,128)S(1)}, f32[2,512,1024]{2,1,0:T(8,128)}) fusion(pred[512,1024]{1,0:T(8,128)(4,1)S(1)} %get-tuple-element.6, bf16[1024,2,264]{0,2,1:T(8,128)(2,1)} %bitcast.85), kind=kOutput, calls=%fused_computation.96 | convolution fusion | flops 188744704 | bytes 5263360 | tf_op jit(solution)/shard_map/sub | solution.py:73
  80.3 3.3 %fusion.24 = bf16[512,2,88]{0,2,1:T(8,128)(2,1)S(1)} fusion(f32[2,512,1024]{2,1,0:T(8,128)} %get-tuple-element.12, f32[2,512]{1,0:T(2,128)S(1)} %get-tuple-element.11, bf16[1024,2,264]{0,2,1:T(8,128)(2,1)} %bitcast.86), kind=kOutput, calls=%fused_computation.37 | convolution fusion | flops 186736640 | bytes 4739072 | tf_op jit(solution)/shard_map/hqk,khd->qhd/dot_general | solution.py:75
  83.8 1.9 fusion.25
  85.9 11.0 %all_to_all.10 = bf16[8,128,176]{1,2,0:T(8,128)(2,1)S(1)} all-to-all(bf16[8,128,176]{1,2,0:T(8,128)(2,1)S(1)} %copy.18), channel_id=1, replica_groups=mesh['dp'=64,'tensor'=8] {'tensor'}, dimensions={0} | all-to-all | bytes 720896 | tf_op jit(solution)/shard_map/all_to_all | solution.py:108
  96.8 3.1 %fusion.84 = (f32[128]{0:T(128)S(1)}, f32[128,1408]{1,0:T(8,128)S(1)}) fusion(bf16[8,128,176]{1,2,0:T(8,128)(2,1)S(1)} %all_to_all.10, bf16[8,176,1408]{2,1,0:T(8,128)(2,1)} %bitcast.74, bf16[128,1408]{1,0:T(8,128)(2,1)S(1)} %copy-done.2), kind=kOutput, calls=%fused_computation.98 | convolution fusion | flops 508411776 | bytes 5407232 | tf_op jit(solution)/shard_map/sqd,sdo->qo/dot_general | solution.py:110
  102.4 107.3 %all-gather.8.cloned.1.call-done = bf16[5632,448]{1,0:T(8,128)(2,1)} async-done(((bf16[88,448]{1,0:T(8,128)(2,1)}), bf16[5632,448]{1,0:T(8,128)(2,1)}) %all-gather.8.cloned.1.call-update) | async-done | bytes 5046288 | tf_op jit(solution)/shard_map/all_gather | solution.py:95
  209.7 32.6 %all-gather.6.cloned.1.call-done = bf16[256,5632]{1,0:T(8,128)(2,1)} async-done(((bf16[32,5632]{1,0:T(8,128)(2,1)}), bf16[256,5632]{1,0:T(8,128)(2,1)}) %all-gather.6.cloned.1.call-update) | async-done | bytes 2883600 | tf_op jit(solution)/shard_map/all_gather | solution.py:114
  242.3 6.0 %convolution_convert_fusion.1 = bf16[512,448]{0,1:T(8,128)(2,1)S(1)} fusion(bf16[256,5632]{1,0:T(8,128)(2,1)} %all-gather.6.cloned.1.call-done, bf16[5632,448]{1,0:T(8,128)(2,1)} %all-gather.8.cloned.1.call-done, s32[256]{0:T(256)S(1)} %multiply_add_fusion, f32[448]{0:T(512)S(1)} %copy-done.9), kind=kOutput, calls=%fused_computation.32 | convolution fusion | flops 1409875968 | bytes 8391424 | tf_op jit(solution)/shard_map/dot_general | solution.py:127
  248.5 47.7 %all_to_all.11 = bf16[64,8,448]{2,1,0:T(8,128)(2,1)S(1)} all-to-all(bf16[64,8,448]{2,1,0:T(8,128)(2,1)S(1)} %bitcast.76), channel_id=1, replica_groups=mesh['dp'=64,'tensor'=8] {'dp'}, dimensions={0} | all-to-all | bytes 917504 | tf_op jit(solution)/shard_map/all_to_all | solution.py:131
  (71 shorter events, 15.6 us)
Async XLA Ops:
  6.5 61.3 %copy-start = (bf16[1408,2,264]{0,2,1:T(8,128)(2,1)S(1)}, bf16[1408,2,264]{0,2,1:T(8,128)(2,1)}, u32[]{:S(2)}) copy-start(bf16[1408,2,264]{0,2,1:T(8,128)(2,1)} %param.14) | copy-start | bytes 4460548
  6.5 47.1 %copy-start.2 = (bf16[128,1408]{1,0:T(8,128)(2,1)S(1)}, bf16[128,1408]{1,0:T(8,128)(2,1)}, u32[]{:S(2)}) copy-start(bf16[128,1408]{1,0:T(8,128)(2,1)} %param.11) | copy-start | bytes 1081348
  6.5 90.3 %all-gather.4.cloned.1.call-start = ((), (), s32[]{:S(2)}) async-start(), calls=%async_computation.2 | async-start | bytes 4460544 | tf_op jit(solution)/shard_map/all_gather | solution.py:96
  7.3 202.4 %all-gather.8.cloned.1.call-start = ((), (), s32[]{:S(2)}) async-start(), calls=%async_computation.4 | async-start | bytes 5857280 | tf_op jit(solution)/shard_map/all_gather | solution.py:95
  7.3 8.3 %collective-permute-start = (bf16[128,1408]{1,0:T(8,128)(2,1)}, bf16[128,1408]{1,0:T(8,128)(2,1)S(1)}, u32[]{:S(2)}, u32[]{:S(2)}) collective-permute-start(bf16[128,1408]{1,0:T(8,128)(2,1)} %param.11), channel_id=1, source_target_pairs={{0,1},{1,2},{2,3},{3,4},{4,5},{5,6},{6,7},{7,0},{8,9},{9,10},{10,1... | collective-permute-start | bytes 1081352 | tf_op jit(solution)/shard_map/ppermute | solution.py:27
  15.6 8.1 %collective-permute-start.1 = (bf16[128,1408]{1,0:T(8,128)(2,1)S(1)}, bf16[128,1408]{1,0:T(8,128)(2,1)S(1)}, u32[]{:S(2)}, u32[]{:S(2)}) collective-permute-start(bf16[128,1408]{1,0:T(8,128)(2,1)S(1)} %collective-permute-done), channel_id=1, source_target_pairs={{0,1},{1,2},{2,3},{3,4},{4,5},{5,6},{6,7},{7,0},{8,9},{9,10},{10,1... | collective-permute-start | bytes 1081352 | tf_op jit(solution)/shard_map/ppermute | solution.py:27
  15.6 10.2 %collective-permute-start.4 = (bf16[128,1408]{1,0:T(8,128)(2,1)}, bf16[128,1408]{1,0:T(8,128)(2,1)}, u32[]{:S(2)}, u32[]{:S(2)}) collective-permute-start(bf16[128,1408]{1,0:T(8,128)(2,1)} %param.11), channel_id=1, source_target_pairs={{1,0},{2,1},{3,2},{4,3},{5,4},{6,5},{7,6},{0,7},{9,8},{10,9},{11,1... | collective-permute-start | bytes 1081352 | tf_op jit(solution)/shard_map/ppermute | solution.py:30
  23.7 8.2 %copy-start.3 = (bf16[128,1408]{1,0:T(8,128)(2,1)}, bf16[128,1408]{1,0:T(8,128)(2,1)S(1)}, u32[]{:S(2)}) copy-start(bf16[128,1408]{1,0:T(8,128)(2,1)S(1)} %collective-permute-done.1) | copy-start | bytes 1081348
  23.7 8.2 %collective-permute-start.2 = (bf16[128,1408]{1,0:T(8,128)(2,1)S(1)}, bf16[128,1408]{1,0:T(8,128)(2,1)}, u32[]{:S(2)}, u32[]{:S(2)}) collective-permute-start(bf16[128,1408]{1,0:T(8,128)(2,1)S(1)} %collective-permute-done.1), channel_id=1, source_target_pairs={{0,1},{1,2},{2,3},{3,4},{4,5},{5,6},{6,7},{7,0},{8,9},{9,10},{10,1... | collective-permute-start | bytes 1081352 | tf_op jit(solution)/shard_map/ppermute | solution.py:27
  23.7 218.6 %all-gather.6.cloned.1.call-start = ((), (), s32[]{:S(2)}) async-start(), calls=%async_computation.3 | async-start | bytes 3244032 | tf_op jit(solution)/shard_map/all_gather | solution.py:114
  25.8 11.2 %collective-permute-start.5 = (bf16[128,1408]{1,0:T(8,128)(2,1)}, bf16[128,1408]{1,0:T(8,128)(2,1)}, u32[]{:S(2)}, u32[]{:S(2)}) collective-permute-start(bf16[128,1408]{1,0:T(8,128)(2,1)} %collective-permute-done.4), channel_id=1, source_target_pairs={{1,0},{2,1},{3,2},{4,3},{5,4},{6,5},{7,6},{0,7},{9,8},{10,9},{11,1... | collective-permute-start | bytes 1081352 | tf_op jit(solution)/shard_map/ppermute | solution.py:30
  31.8 15.8 %collective-permute-start.3 = (bf16[128,1408]{1,0:T(8,128)(2,1)}, bf16[128,1408]{1,0:T(8,128)(2,1)}, u32[]{:S(2)}, u32[]{:S(2)}) collective-permute-start(bf16[128,1408]{1,0:T(8,128)(2,1)} %collective-permute-done.2), channel_id=1, source_target_pairs={{0,1},{1,2},{2,3},{3,4},{4,5},{5,6},{6,7},{7,0},{8,9},{9,10},{10,1... | collective-permute-start | bytes 1081352 | tf_op jit(solution)/shard_map/ppermute | solution.py:27
  36.9 21.0 %collective-permute-start.6 = (bf16[128,1408]{1,0:T(8,128)(2,1)}, bf16[128,1408]{1,0:T(8,128)(2,1)S(1)}, u32[]{:S(2)}, u32[]{:S(2)}) collective-permute-start(bf16[128,1408]{1,0:T(8,128)(2,1)} %collective-permute-done.5), channel_id=1, source_target_pairs={{1,0},{2,1},{3,2},{4,3},{5,4},{6,5},{7,6},{0,7},{9,8},{10,9},{11,1... | collective-permute-start | bytes 1081352 | tf_op jit(solution)/shard_map/ppermute | solution.py:30
  63.1 2.7 copy-start.1
  63.1 3.6 %copy-start.5 = (f32[1408]{0:T(1024)S(1)}, f32[1408]{0:T(1024)}, u32[]{:S(2)}) copy-start(f32[1408]{0:T(1024)} %param.13) | copy-start | bytes 16900
  63.1 3.6 %copy-start.6 = (f32[1408]{0:T(1024)S(1)}, f32[1408]{0:T(1024)}, u32[]{:S(2)}) copy-start(f32[1408]{0:T(1024)} %param.12) | copy-start | bytes 16900
  80.3 3.6 %copy-start.10 = (f32[2,512,1024]{2,1,0:T(8,128)S(1)}, f32[2,512,1024]{2,1,0:T(8,128)}, u32[]{:S(2)}) copy-start(f32[2,512,1024]{2,1,0:T(8,128)} %get-tuple-element.10) | copy-start | bytes 12582916
  96.8 3.3 %copy-start.7 = (f32[1408]{0:T(1024)S(1)}, f32[1408]{0:T(1024)}, u32[]{:S(2)}) copy-start(f32[1408]{0:T(1024)} %param.17) | copy-start | bytes 16900
  96.8 3.3 %copy-start.8 = (f32[1408]{0:T(1024)S(1)}, f32[1408]{0:T(1024)}, u32[]{:S(2)}) copy-start(f32[1408]{0:T(1024)} %param.16) | copy-start | bytes 16900
  96.8 4.6 %copy-start.4 = (s32[256,1]{0,1:T(1,128)S(1)}, s32[256,1]{0,1:T(1,128)}, u32[]{:S(2)}) copy-start(s32[256,1]{0,1:T(1,128)} %param.21) | copy-start | bytes 3076
  99.9 142.4 %copy-start.9 = (f32[448]{0:T(512)S(1)}, f32[448]{0:T(512)}, u32[]{:S(2)}) copy-start(f32[448]{0:T(512)} %param.19) | copy-start | bytes 5380
Sparse Core Ops, SparseCore 0:
  9.5 47.0 all-gather.3
  59.5 150.1 all-gather.7
  211.8 30.4 all-gather.5
